TPU v7x, 512 devices: a whole 4x4x16 slice. The times are simulated.
512 devices in a mesh: ctx: 32 (over z_hi, y, x), exp: 16 (over z_lo, core).
Axes of the slice: x: 4, y: 4, z: 16 (z_hi: 2, z_lo: 8; z = z_hi * 8 + z_lo), core: 2. Of those that a mesh axis runs over, the one named last changes fastest.
Arguments:
- hidden_in: bfloat16 [4096, 2880], P('ctx'), may hold values from -6 to 6
- query_input: bfloat16 [4096, 2048], P('ctx', 'exp'), may hold values from -16 to 16
- key_heads_input: bfloat16 [4096, 256], P('ctx'), may hold values from -16 to 16
- value_heads_input: bfloat16 [4096, 256], P('ctx'), may hold values from -6 to 6
- sink_logits: float32 [32], P('exp'), may hold values from 0 to 4
- out_proj: bfloat16 [2048, 2880], P('exp'), may hold values from -0.125 to 0.125
- norm_gain: float32 [2880], replicated, may hold values from 0.5 to 1.5
- expert_ids: int32 [4096, 4], P('ctx'), may hold values from 0 to 31, all different within a row; in each aligned block of 128 rows (0 to 127, 128 to 255, ...) at most 20 rows name the same one
- expert_gates: float32 [4096, 4], P('ctx'), may hold values from 0.1 to 1
- gate_up: bfloat16 [32, 2880, 2, 2880], P('ctx', None, None, 'exp'), may hold values from -0.109375 to 0.109375
- down_proj: bfloat16 [32, 2880, 2880], P('ctx', 'exp'), may hold values from -0.109375 to 0.109375
Outputs:
- layer_out: bfloat16 [4096, 2880], P('ctx', 'exp')
Inputs may be any that keep to these rules, and one draw needn't show every extreme that they name: `expert_ids`: each token names 4 different experts; within the 128 tokens of one device no expert is named by more than 20 tokens.
All inputs are finite; a program needn't handle non-finite values.
Results may differ from a plain program's by a relative error of at most 0.02.
Values may be sent and summed in bfloat16 or wider, within the bound.
No kernel may reach another device: no remote copies, remote signals or barrier semaphores. Data moves between devices by JAX's collectives and lax.ppermute only.
A program may use at most 64 MiB of HBM per device.

v0:
```python
import math
import jax
import jax.numpy as jnp
import numpy as np
from jax import lax
from jax.sharding import PartitionSpec as P

D = 2880
QUERY_HEADS = 32
KEY_VALUE_HEADS = 4
HEAD_SIZE = 64
yarn_base = 150000.0
yarn_factor = 32.0
yarn_initial = 4096.0
beta_fast = 32.0
beta_slow = 1.0
neg_large = -1e30


def yarn_frequencies(head_dim):
    half_dim = head_dim // 2

    def correction(rotations):
        return (
            head_dim
            * math.log(yarn_initial / (rotations * 2.0 * math.pi))
            / (2.0 * math.log(yarn_base))
        )

    lower_dim = max(math.floor(correction(beta_fast)), 0)
    upper_dim = min(math.ceil(correction(beta_slow)), head_dim - 1)
    extrap_freq = 1.0 / yarn_base ** (np.arange(0, head_dim, 2) / head_dim)
    interp_freq = extrap_freq / yarn_factor
    ramp_part = np.clip((np.arange(half_dim) - lower_dim) / (upper_dim - lower_dim), 0.0, 1.0)
    extrap_share = 1.0 - ramp_part
    return (interp_freq * (1.0 - extrap_share) + extrap_freq * extrap_share).astype(np.float32)


def rotate_with_yarn(heads_in, token_positions):
    head_dim = heads_in.shape[-1]
    freqs = jnp.asarray(yarn_frequencies(head_dim))
    angles = token_positions.astype(jnp.float32)[:, None] * freqs[None, :]
    factor = 0.1 * math.log(yarn_factor) + 1.0
    cosine = (jnp.cos(angles) * factor)[:, None, :]
    sine = (jnp.sin(angles) * factor)[:, None, :]
    first_half = heads_in[..., : head_dim // 2]
    second_half = heads_in[..., head_dim // 2 :]
    return jnp.concatenate(
        [first_half * cosine - second_half * sine, second_half * cosine + first_half * sine],
        axis=-1,
    )


def route_slots(ids_block, n_experts):
    flat_ids = ids_block.reshape(-1)
    onehot = (flat_ids[:, None] == jnp.arange(n_experts, dtype=jnp.int32)[None, :]).astype(
        jnp.int32
    )
    ranks = jnp.cumsum(onehot, axis=0) - onehot
    return jnp.sum(ranks * onehot, axis=1).reshape(ids_block.shape)


def per_device(
    hidden_in,
    query_input,
    key_heads_input,
    value_heads_input,
    sink_logits,
    out_proj,
    norm_gain,
    expert_ids,
    expert_gates,
    gate_up,
    down_proj,
):
    tok_rows = hidden_in.shape[0]
    ctx_count = lax.axis_size("ctx")
    exp_count = lax.axis_size("exp")
    local_heads = query_input.shape[1] // HEAD_SIZE
    token_positions = lax.axis_index("ctx") * tok_rows + jnp.arange(tok_rows, dtype=jnp.int32)
    q_rot = rotate_with_yarn(
        query_input.astype(jnp.float32).reshape(tok_rows, local_heads, HEAD_SIZE), token_positions
    ).astype(jnp.bfloat16)
    shared_key_head = lax.axis_index("exp") * local_heads // (QUERY_HEADS // KEY_VALUE_HEADS)
    key_block = lax.dynamic_slice_in_dim(key_heads_input, shared_key_head * HEAD_SIZE, HEAD_SIZE, 1)
    value_block = lax.dynamic_slice_in_dim(
        value_heads_input, shared_key_head * HEAD_SIZE, HEAD_SIZE, 1
    )
    key_rot = (
        rotate_with_yarn(
            key_block.astype(jnp.float32).reshape(tok_rows, 1, HEAD_SIZE), token_positions
        )
        .reshape(tok_rows, HEAD_SIZE)
        .astype(jnp.bfloat16)
    )
    key_value = jnp.concatenate([key_rot, value_block], axis=1)
    score_scale = 1.0 / math.sqrt(HEAD_SIZE)
    block_part = lax.all_gather(key_value, "ctx", axis=0, tiled=True)
    run_max = jnp.broadcast_to(sink_logits[:, None], (local_heads, tok_rows))
    run_total = jnp.ones((local_heads, tok_rows), jnp.float32)
    run_sum = jnp.zeros((local_heads, tok_rows, HEAD_SIZE), jnp.float32)
    key_count = block_part.shape[0]
    key_part = block_part[:, :HEAD_SIZE]
    value_part = block_part[:, HEAD_SIZE:].astype(jnp.float32)
    scores = (
        jnp.einsum("rhd,kd->hrk", q_rot, key_part, preferred_element_type=jnp.float32) * score_scale
    )
    key_pos = jnp.arange(key_count, dtype=jnp.int32)
    visible = token_positions[:, None] >= key_pos[None, :]
    scores = jnp.where(visible[None, :, :], scores, neg_large)
    new_max = jnp.maximum(run_max, jnp.max(scores, axis=2))
    weights = jnp.exp(scores - new_max[:, :, None])
    factor = jnp.exp(run_max - new_max)
    run_total = run_total * factor + jnp.sum(weights, axis=2)
    run_sum = run_sum * factor[:, :, None] + jnp.einsum(
        "hrk,kd->hrd", weights, value_part, precision=lax.Precision.HIGHEST
    )
    run_max, run_total, run_sum = (new_max, run_total, run_sum)
    attended = (
        (run_sum / run_total[:, :, None])
        .transpose(1, 0, 2)
        .reshape(tok_rows, local_heads * HEAD_SIZE)
        .astype(jnp.bfloat16)
    )
    head_part = jnp.dot(attended, out_proj, preferred_element_type=jnp.float32)
    residual = hidden_in.astype(jnp.float32) + lax.psum(
        head_part.astype(jnp.bfloat16), "exp"
    ).astype(jnp.float32)
    mean_square = jnp.mean(residual * residual, axis=1, keepdims=True)
    normed = (residual * lax.rsqrt(mean_square + 1e-05) * norm_gain[None, :]).astype(jnp.bfloat16)
    exp_local = gate_up.shape[0]
    n_experts = exp_local * ctx_count
    top_count = expert_ids.shape[1]
    capacity = max(2, tok_rows * top_count * 5 // (4 * n_experts))
    slot_index = route_slots(expert_ids, n_experts)
    dest_row = expert_ids * capacity + slot_index
    spread_rows = jnp.broadcast_to(normed[:, None, :], (tok_rows, top_count, D)).reshape(
        tok_rows * top_count, D
    )
    send_rows = (
        jnp.zeros((n_experts * capacity, D), jnp.bfloat16).at[dest_row.reshape(-1)].set(spread_rows)
    )
    bucket_rows = ctx_count * capacity
    unit_count = gate_up.shape[-1]
    col_width = D // exp_count
    weights_flat = gate_up.reshape(exp_local, D, 2 * unit_count)
    received = lax.all_to_all(
        send_rows.reshape(ctx_count, exp_local * capacity, D),
        "ctx",
        split_axis=0,
        concat_axis=0,
        tiled=True,
    )
    expert_rows = (
        received.reshape(ctx_count, exp_local, capacity, D)
        .transpose(1, 0, 2, 3)
        .reshape(exp_local, bucket_rows, D)
    )
    gate_up_out = jnp.einsum(
        "erd,edf->erf", expert_rows, weights_flat, preferred_element_type=jnp.float32
    )
    gate_up_out = gate_up_out.reshape(exp_local, bucket_rows, 2, unit_count)
    gate_value = gate_up_out[:, :, 0]
    up_value = gate_up_out[:, :, 1]
    activated = ((up_value + 1.0) * gate_value * jax.nn.sigmoid(1.702 * gate_value)).astype(
        jnp.bfloat16
    )
    partial_value = jnp.einsum(
        "erf,efd->erd", activated, down_proj, preferred_element_type=jnp.float32
    )
    partial_rounded = partial_value.astype(jnp.bfloat16)
    outgoing = partial_rounded.reshape(exp_local, ctx_count, capacity, D).transpose(1, 0, 2, 3)
    returned = lax.all_to_all(
        outgoing.reshape(ctx_count, exp_local * capacity, D),
        "ctx",
        split_axis=0,
        concat_axis=0,
        tiled=True,
    )
    picked_rows = returned.reshape(n_experts * capacity, D)[dest_row]
    gated = jnp.sum(expert_gates[:, :, None] * picked_rows.astype(jnp.float32), axis=1)
    moe_cols = lax.psum_scatter(
        gated.astype(jnp.bfloat16), "exp", scatter_dimension=1, tiled=True
    ).astype(jnp.float32)
    residual_cols = lax.dynamic_slice_in_dim(
        residual, lax.axis_index("exp") * col_width, col_width, 1
    )
    return (residual_cols + moe_cols).astype(jnp.bfloat16)


def solution(mesh):
    placed = (
        P("ctx", None),
        P("ctx", "exp"),
        P("ctx", None),
        P("ctx", None),
        P("exp"),
        P("exp", None),
        P(),
        P("ctx", None),
        P("ctx", None),
        P("ctx", None, None, "exp"),
        P("ctx", "exp", None),
    )
    return jax.shard_map(
        per_device, mesh=mesh, in_specs=placed, out_specs=P("ctx", "exp"), check_vma=False
    )
```

profile of v0, /device:TPU:8, one launch (start us, length us, event | category | flops | bytes accessed | tf_op | source)
XLA Modules:
  0.0 880.9 jit_solution(616412392526156827)
XLA Ops:
  6.5 1.0 constant_dynamic-slice_fusion
  7.7 0.8 fusion.35
  8.6 0.6 pad_maximum_fusion
  9.2 0.8 copy.51
  10.1 0.8 copy.54
  11.0 0.8 fusion.41
  11.8 0.3 iota_compare_fusion
  12.2 119.5 %all-gather.2.cloned.1.call-done = bf16[4096,128]{0,1:T(8,128)(2,1)} async-done(((bf16[128,128]{0,1:T(8,128)(2,1)}), bf16[4096,128]{0,1:T(8,128)(2,1)}) %all-gather.2.cloned.1.call-update) | async-done | bytes 1048592 | tf_op jit(solution)/shard_map/all_gather | solution.py:98
  131.7 2.0 fusion.47
  133.8 0.6 fusion.5
  134.4 2.1 fusion.16
  136.5 1.2 convolution_convert_fusion.1
  137.9 1.3 reduce-window.6
  139.2 0.2 slice_reduce_fusion
  139.8 0.1 copy.58
  139.9 0.1 reshape.374
  140.0 186.8 %all-reduce.4.cloned.1.call-done = bf16[128,2880]{0,1:T(8,128)(2,1)} async-done(((bf16[128,2880]{0,1:T(8,128)(2,1)}), bf16[128,2880]{0,1:T(8,128)(2,1)}) %all-reduce.4.cloned.1.call-update) | async-done | bytes 737296 | tf_op jit(solution)/shard_map/psum | solution.py:126
  326.8 1.5 multiply_reduce_fusion.1
  328.3 2.7 multiply_convert_fusion
  331.0 0.4 copy.59
  331.4 2.4 broadcast_in_dim.27
  333.8 5.6 reshape.397
  339.4 8.4 scatter_custom_fusion
  347.7 6.4 reshape.376
  354.1 17.0 %all-to-all-start = ((bf16[32,20,2880]{2,1,0:T(8,128)(2,1)}), bf16[32,20,2880]{2,1,0:T(8,128)(2,1)}, u32[]{:S(2)}, u32[]{:S(2)}) async-start(bf16[32,20,2880]{2,1,0:T(8,128)(2,1)} %reshape.376), calls=%async_computation | async-start | bytes 9043968 | tf_op jit(solution)/shard_map/all_to_all | solution.py:147
  371.1 1.8 copy.60
  372.9 2.3 reshape.378
  375.1 2.1 dot_general.28
  377.2 174.9 %all-to-all-done = bf16[32,20,2880]{2,1,0:T(8,128)(2,1)} async-done(((bf16[32,20,2880]{2,1,0:T(8,128)(2,1)}), bf16[32,20,2880]{2,1,0:T(8,128)(2,1)}, u32[]{:S(2)}, u32[]{:S(2)}) %all-to-all-start) | async-done | bytes 3686432 | tf_op jit(solution)/shard_map/all_to_all | solution.py:147
  552.2 6.6 reshape.377
  558.7 4.0 fusion.10
  562.8 3.3 convolution_convert_fusion
  566.1 6.2 copy.62
  572.3 6.4 reshape_transpose_reshape.4
  578.6 122.0 %all-to-all-start.1 = ((bf16[32,20,2880]{2,1,0:T(8,128)(2,1)}), bf16[32,20,2880]{2,1,0:T(8,128)(2,1)}, u32[]{:S(2)}, u32[]{:S(2)}) async-start(bf16[32,20,2880]{2,1,0:T(8,128)(2,1)} %reshape_transpose_reshape.4), calls=%async_computation.1 | async-start | bytes 9043968 | tf_op jit(solution)/shard_map/all_to_all | solution.py:173
  700.7 0.1 copy.63
  700.9 0.1 copy.53
  701.0 80.2 %all-to-all-done.1 = bf16[32,20,2880]{2,1,0:T(8,128)(2,1)} async-done(((bf16[32,20,2880]{2,1,0:T(8,128)(2,1)}), bf16[32,20,2880]{2,1,0:T(8,128)(2,1)}, u32[]{:S(2)}, u32[]{:S(2)}) %all-to-all-start.1) | async-done | bytes 3686432 | tf_op jit(solution)/shard_map/all_to_all | solution.py:173
  781.2 6.6 reshape.380
  787.8 9.3 %gather_fusion = bf16[512,2880]{1,0:T(8,128)(2,1)} fusion(bf16[640,2880]{1,0:T(8,128)(2,1)} %reshape.380, s32[1024]{0:T(1024)S(1)} %pad_clamp_fusion), kind=kCustom, calls=%fused_computation | custom fusion | bytes 5900288 | tf_op jit(solution)/shard_map/gather | solution.py:180
  797.1 6.6 reshape.403
  803.7 7.1 multiply_reduce_fusion
  810.8 0.4 copy.64
  811.2 57.7 %fusion = bf16[128,192]{0,1:T(8,128)(2,1)S(1)} fusion(bf16[128,2880]{0,1:T(8,128)(2,1)S(1)} %copy.64), kind=kCustom, calls=%all-reduce-scatter | all-reduce-scatter fusion | flops 393217 | bytes 788480
  868.9 1.3 collective-permute-start
  870.2 1.3 dynamic-slice.4
  872.2 0.4 concatenate.14
  872.5 1.5 add_convert_fusion
  (46 shorter events, 1.2 us)
Async XLA Ops:
  6.5 556.2 %copy-start = (bf16[1,180,2880]{2,1,0:T(8,128)(2,1)S(1)}, bf16[1,180,2880]{2,1,0:T(8,128)(2,1)}, u32[]{:S(2)}) copy-start(bf16[1,180,2880]{2,1,0:T(8,128)(2,1)} %param.23) | copy-start | bytes 3110404
  6.5 125.1 %all-gather.2.cloned.1.call-start = ((), (), s32[]{:S(2)}) async-start(), calls=%async_computation.2 | async-start | bytes 1081344 | tf_op jit(solution)/shard_map/all_gather | solution.py:98
  7.6 126.1 %copy-start.8 = (f32[2]{0:T(128)S(1)}, f32[2]{0:T(128)}, u32[]{:S(2)}) copy-start(f32[2]{0:T(128)} %param.17) | copy-start | bytes 28
  9.2 317.6 %all-reduce.4.cloned.1.call-start = ((), (), s32[]{:S(2)}) async-start(), calls=%async_computation.3 | async-start | bytes 1474560 | tf_op jit(solution)/shard_map/psum | solution.py:126
  131.7 2.7 copy-start.4
  133.8 2.7 copy-start.3
  134.4 5.4 copy-start.6
  134.4 192.4 %copy-start.2 = (bf16[128,2880]{0,1:T(8,128)(2,1)S(1)}, bf16[128,2880]{0,1:T(8,128)(2,1)}, u32[]{:S(2)}) copy-start(bf16[128,2880]{0,1:T(8,128)(2,1)} %param.13) | copy-start | bytes 2211844
  134.4 193.9 %copy-start.5 = (f32[2880]{0:T(1024)S(1)}, f32[2880]{0:T(1024)}, u32[]{:S(2)}) copy-start(f32[2880]{0:T(1024)} %param.19) | copy-start | bytes 34564
  354.1 198.1 %all-to-all-start = ((bf16[32,20,2880]{2,1,0:T(8,128)(2,1)}), bf16[32,20,2880]{2,1,0:T(8,128)(2,1)}, u32[]{:S(2)}, u32[]{:S(2)}) async-start(bf16[32,20,2880]{2,1,0:T(8,128)(2,1)} %reshape.376), calls=%async_computation | async-start | bytes 9043968 | tf_op jit(solution)/shard_map/all_to_all | solution.py:147
  578.6 122.2 %copy-start.7 = (f32[128,4]{0,1:T(4,128)S(1)}, f32[128,4]{0,1:T(4,128)}, u32[]{:S(2)}) copy-start(f32[128,4]{0,1:T(4,128)} %param.21) | copy-start | bytes 6148
  578.6 202.6 %all-to-all-start.1 = ((bf16[32,20,2880]{2,1,0:T(8,128)(2,1)}), bf16[32,20,2880]{2,1,0:T(8,128)(2,1)}, u32[]{:S(2)}, u32[]{:S(2)}) async-start(bf16[32,20,2880]{2,1,0:T(8,128)(2,1)} %reshape_transpose_reshape.4), calls=%async_computation.1 | async-start | bytes 9043968 | tf_op jit(solution)/shard_map/all_to_all | solution.py:173
  797.1 77.0 %copy-start.1 = (bf16[1,180,2880]{2,1,0:T(8,128)(2,1)S(1)}, bf16[1,180,2880]{2,1,0:T(8,128)(2,1)}, u32[]{:S(2)}) copy-start(bf16[1,180,2880]{2,1,0:T(8,128)(2,1)} %param.23) | copy-start | bytes 3110404
  868.9 3.2 collective-permute-start
Sparse Core Ops, SparseCore 0:
  11.4 120.1 all-gather.1
  137.8 188.8 all-reduce.3
where the time goes:
time: 883 us; the launch traced here: 881 us
  waiting for transfers between devices  561 us (64%)
  starting transfers between devices  140 us (16%)
  local copies, waits for them, and re-layouts  76.8 us (9%)
  blocking collectives  57.7 us (7%)
  other arithmetic  17.7 us (2%)
  between operations  14.3 us (2%)
  matrix products  12.6 us (1%)
    psum x1, waiting for transfers between devices, per_device(): lax.psum(head_part.astype(jnp.bfloat16), 'exp').astype(jnp.float32)  187 us
    all_to_all x1, waiting for transfers between devices, per_device(): lax.all_to_all(send_rows.reshape(ctx_count, exp_local * capacity, D), 'ct...  175 us
    all_to_all x1, starting transfers between devices, per_device(): lax.all_to_all(outgoing.reshape(ctx_count, exp_local * capacity, D), 'ctx...  122 us
    all_gather x1, waiting for transfers between devices, per_device(): block_part = lax.all_gather(key_value, 'ctx', axis=0, tiled=True)  119 us
    all_to_all x1, waiting for transfers between devices, per_device(): lax.all_to_all(outgoing.reshape(ctx_count, exp_local * capacity, D), 'ctx...  80.2 us
    unnamed x1, blocking collectives  57.7 us
  transfers between devices with their start and end apart: 5, of which 4 were waited for; matrix products, arithmetic and copies ran while one was open for 1% of the time, Pallas kernels for 0%

commit v1 on v0

--- a/solution.py
+++ b/solution.py
@@ -15,6 +15,11 @@
 beta_fast = 32.0
 beta_slow = 1.0
 neg_large = -1e30
+
+
+def all_by_exchange(shard, axis, along):
+    sent = jnp.stack([shard] * lax.axis_size(axis))
+    return jnp.concatenate(lax.all_to_all(sent, axis, 0, 0), axis=along)
 
 
 def yarn_frequencies(head_dim):
@@ -95,7 +100,7 @@
     )
     key_value = jnp.concatenate([key_rot, value_block], axis=1)
     score_scale = 1.0 / math.sqrt(HEAD_SIZE)
-    block_part = lax.all_gather(key_value, "ctx", axis=0, tiled=True)
+    block_part = all_by_exchange(key_value, "ctx", 0)
     run_max = jnp.broadcast_to(sink_logits[:, None], (local_heads, tok_rows))
     run_total = jnp.ones((local_heads, tok_rows), jnp.float32)
     run_sum = jnp.zeros((local_heads, tok_rows, HEAD_SIZE), jnp.float32)

time: 883 us -> 839 us (0.950)
  waiting for transfers between devices: 561 us -> 500 us
  starting transfers between devices: 140 us -> 161 us
    all_gather x1 -> x0, waiting for transfers between devices: 119 us -> none  [per_device(): block_part = lax.all_gather(key_value, 'ctx', axis=0, tiled=True)]
    psum x1, waiting for transfers between devices: 187 us -> 217 us  [per_device(): lax.psum(head_part.astype(jnp.bfloat16), 'exp').astype(jnp.float32)]
    all_to_all x0 -> x1, waiting for transfers between devices: none -> 27.8 us  [all_by_exchange(): return jnp.concatenate(lax.all_to_all(sent, axis, 0, 0), axis=along)]
    all_to_all x0 -> x1, starting transfers between devices: none -> 20.8 us  [all_by_exchange(): return jnp.concatenate(lax.all_to_all(sent, axis, 0, 0), axis=along)]
where the time goes in v1:
time: 839 us; the launch traced here: 838 us
  waiting for transfers between devices  500 us (60%)
  starting transfers between devices  161 us (19%)
  local copies, waits for them, and re-layouts  76.8 us (9%)
  blocking collectives  57.7 us (7%)
  other arithmetic  16.4 us (2%)
  between operations  14.4 us (2%)
  matrix products  11.5 us (1%)
    psum x1, waiting for transfers between devices, per_device(): lax.psum(head_part.astype(jnp.bfloat16), 'exp').astype(jnp.float32)  217 us
    all_to_all x1, waiting for transfers between devices, per_device(): lax.all_to_all(send_rows.reshape(ctx_count, exp_local * capacity, D), 'ct...  175 us
    all_to_all x1, starting transfers between devices, per_device(): lax.all_to_all(outgoing.reshape(ctx_count, exp_local * capacity, D), 'ctx...  122 us
    all_to_all x1, waiting for transfers between devices, per_device(): lax.all_to_all(outgoing.reshape(ctx_count, exp_local * capacity, D), 'ctx...  80.3 us
    unnamed x1, blocking collectives  57.7 us
    all_to_all x1, waiting for transfers between devices, all_by_exchange(): return jnp.concatenate(lax.all_to_all(sent, axis, 0, 0), axis=along)  27.8 us
    all_to_all x1, starting transfers between devices, all_by_exchange(): return jnp.concatenate(lax.all_to_all(sent, axis, 0, 0), axis=along)  20.8 us
    all_to_all x1, starting transfers between devices, per_device(): lax.all_to_all(send_rows.reshape(ctx_count, exp_local * capacity, D), 'ct...  17 us
  transfers between devices with their start and end apart: 5, of which 4 were waited for; matrix products, arithmetic and copies ran while one was open for 1% of the time, Pallas kernels for 0%

profile of v1, /device:TPU:8, one launch (start us, length us, event | category | flops | bytes accessed | tf_op | source)
XLA Modules:
  0.0 837.6 jit_solution(12530415360333547262)
XLA Ops:
  6.5 1.0 constant_dynamic-slice_fusion
  7.7 0.8 fusion.35
  8.6 1.2 stack.2
  9.8 20.8 %all-to-all-start = ((bf16[32,128,128]{1,2,0:T(8,128)(2,1)}), bf16[32,128,128]{1,2,0:T(8,128)(2,1)S(1)}, u32[]{:S(2)}, u32[]{:S(2)}) async-start(bf16[32,128,128]{1,2,0:T(8,128)(2,1)} %stack.2), calls=%async_computation | async-start | bytes 2097152 | tf_op jit(solution)/shard_map/all_to_all | solution.py:22
  30.8 0.1 copy.53
  31.0 0.1 fusion.41
  31.2 0.3 iota_compare_fusion
  31.5 27.8 %all-to-all-done = bf16[32,128,128]{1,2,0:T(8,128)(2,1)S(1)} async-done(((bf16[32,128,128]{1,2,0:T(8,128)(2,1)}), bf16[32,128,128]{1,2,0:T(8,128)(2,1)S(1)}, u32[]{:S(2)}, u32[]{:S(2)}) %all-to-all-start) | async-done | bytes 1048608 | tf_op jit(solution)/shard_map/all_to_all | solution.py:22
  59.4 0.1 copy_bitcast_fusion
  59.5 0.9 fusion.47
  60.5 0.6 fusion.5
  61.1 2.1 fusion.16
  63.2 1.2 convolution_convert_fusion.1
  64.6 1.3 reduce-window.6
  65.9 0.2 slice_reduce_fusion
  66.5 0.1 copy.57
  66.7 216.7 %all-reduce.4.cloned.1.call-done = bf16[128,2880]{0,1:T(8,128)(2,1)} async-done(((bf16[128,2880]{0,1:T(8,128)(2,1)}), bf16[128,2880]{0,1:T(8,128)(2,1)}) %all-reduce.4.cloned.1.call-update) | async-done | bytes 737296 | tf_op jit(solution)/shard_map/psum | solution.py:131
  283.5 1.5 multiply_reduce_fusion.1
  285.0 2.7 multiply_convert_fusion
  287.7 0.4 copy.58
  288.1 2.4 broadcast_in_dim.27
  290.5 5.6 reshape.403
  296.1 8.4 scatter_custom_fusion
  304.4 6.4 reshape.382
  310.8 17.0 %all-to-all-start.1 = ((bf16[32,20,2880]{2,1,0:T(8,128)(2,1)}), bf16[32,20,2880]{2,1,0:T(8,128)(2,1)}, u32[]{:S(2)}, u32[]{:S(2)}) async-start(bf16[32,20,2880]{2,1,0:T(8,128)(2,1)} %reshape.382), calls=%async_computation.1 | async-start | bytes 9043968 | tf_op jit(solution)/shard_map/all_to_all | solution.py:152
  327.8 1.8 copy.59
  329.6 2.3 reshape.384
  331.8 2.1 dot_general.28
  333.9 174.9 %all-to-all-done.1 = bf16[32,20,2880]{2,1,0:T(8,128)(2,1)} async-done(((bf16[32,20,2880]{2,1,0:T(8,128)(2,1)}), bf16[32,20,2880]{2,1,0:T(8,128)(2,1)}, u32[]{:S(2)}, u32[]{:S(2)}) %all-to-all-start.1) | async-done | bytes 3686432 | tf_op jit(solution)/shard_map/all_to_all | solution.py:152
  508.9 6.6 reshape.383
  515.4 4.0 fusion.10
  519.5 3.3 convolution_convert_fusion
  522.8 6.2 copy.61
  529.0 6.4 reshape_transpose_reshape.4
  535.3 122.0 %all-to-all-start.2 = ((bf16[32,20,2880]{2,1,0:T(8,128)(2,1)}), bf16[32,20,2880]{2,1,0:T(8,128)(2,1)}, u32[]{:S(2)}, u32[]{:S(2)}) async-start(bf16[32,20,2880]{2,1,0:T(8,128)(2,1)} %reshape_transpose_reshape.4), calls=%async_computation.2 | async-start | bytes 9043968 | tf_op jit(solution)/shard_map/all_to_all | solution.py:178
  657.3 0.1 copy.62
  657.6 0.1 copy.52
  657.7 80.3 %all-to-all-done.2 = bf16[32,20,2880]{2,1,0:T(8,128)(2,1)} async-done(((bf16[32,20,2880]{2,1,0:T(8,128)(2,1)}), bf16[32,20,2880]{2,1,0:T(8,128)(2,1)}, u32[]{:S(2)}, u32[]{:S(2)}) %all-to-all-start.2) | async-done | bytes 3686432 | tf_op jit(solution)/shard_map/all_to_all | solution.py:178
  738.0 6.6 reshape.386
  744.5 9.3 %gather_fusion = bf16[512,2880]{1,0:T(8,128)(2,1)} fusion(bf16[640,2880]{1,0:T(8,128)(2,1)} %reshape.386, s32[1024]{0:T(1024)S(1)} %pad_clamp_fusion), kind=kCustom, calls=%fused_computation | custom fusion | bytes 5900288 | tf_op jit(solution)/shard_map/gather | solution.py:185
  753.8 6.6 reshape.409
  760.4 7.1 multiply_reduce_fusion
  767.5 0.4 copy.63
  767.9 57.7 %fusion = bf16[128,192]{0,1:T(8,128)(2,1)S(1)} fusion(bf16[128,2880]{0,1:T(8,128)(2,1)S(1)} %copy.63), kind=kCustom, calls=%all-reduce-scatter | all-reduce-scatter fusion | flops 393217 | bytes 788480
  825.6 1.3 collective-permute-start
  826.9 1.3 dynamic-slice.4
  828.8 0.4 concatenate.14
  829.2 1.5 add_convert_fusion
  (49 shorter events, 1.4 us)
Async XLA Ops:
  6.5 512.9 %copy-start = (bf16[1,180,2880]{2,1,0:T(8,128)(2,1)S(1)}, bf16[1,180,2880]{2,1,0:T(8,128)(2,1)}, u32[]{:S(2)}) copy-start(bf16[1,180,2880]{2,1,0:T(8,128)(2,1)} %param.23) | copy-start | bytes 3110404
  6.5 24.5 %copy-start.7 = (f32[32]{0:T(128)S(1)}, f32[32]{0:T(128)}, u32[]{:S(2)}) copy-start(f32[32]{0:T(128)} %constant.73.clone) | copy-start | bytes 388
  6.5 24.1 %copy-start.4 = (bf16[128,128]{1,0:T(8,128)(2,1)S(1)}, bf16[128,128]{1,0:T(8,128)(2,1)}, u32[]{:S(2)}) copy-start(bf16[128,128]{1,0:T(8,128)(2,1)} %param.14) | copy-start | bytes 98308
  6.5 24.2 %copy-start.6 = (s32[128,4]{0,1:T(4,128)S(1)}, s32[128,4]{0,1:T(4,128)}, u32[]{:S(2)}) copy-start(s32[128,4]{0,1:T(4,128)} %param.20) | copy-start | bytes 6148
  9.8 49.6 %all-to-all-start = ((bf16[32,128,128]{1,2,0:T(8,128)(2,1)}), bf16[32,128,128]{1,2,0:T(8,128)(2,1)S(1)}, u32[]{:S(2)}, u32[]{:S(2)}) async-start(bf16[32,128,128]{1,2,0:T(8,128)(2,1)} %stack.2), calls=%async_computation | async-start | bytes 2097152 | tf_op jit(solution)/shard_map/all_to_all | solution.py:22
  30.6 252.9 %all-reduce.4.cloned.1.call-start = ((), (), s32[]{:S(2)}) async-start(), calls=%async_computation.3 | async-start | bytes 1474560 | tf_op jit(solution)/shard_map/psum | solution.py:131
  31.5 28.9 %copy-start.9 = (f32[2]{0:T(128)S(1)}, f32[2]{0:T(128)}, u32[]{:S(2)}) copy-start(f32[2]{0:T(128)} %param.17) | copy-start | bytes 28
  60.5 2.7 copy-start.3
  61.1 222.4 %copy-start.2 = (bf16[128,2880]{0,1:T(8,128)(2,1)S(1)}, bf16[128,2880]{0,1:T(8,128)(2,1)}, u32[]{:S(2)}) copy-start(bf16[128,2880]{0,1:T(8,128)(2,1)} %param.13) | copy-start | bytes 2211844
  61.1 223.9 %copy-start.5 = (f32[2880]{0:T(1024)S(1)}, f32[2880]{0:T(1024)}, u32[]{:S(2)}) copy-start(f32[2880]{0:T(1024)} %param.19) | copy-start | bytes 34564
  310.8 198.1 %all-to-all-start.1 = ((bf16[32,20,2880]{2,1,0:T(8,128)(2,1)}), bf16[32,20,2880]{2,1,0:T(8,128)(2,1)}, u32[]{:S(2)}, u32[]{:S(2)}) async-start(bf16[32,20,2880]{2,1,0:T(8,128)(2,1)} %reshape.382), calls=%async_computation.1 | async-start | bytes 9043968 | tf_op jit(solution)/shard_map/all_to_all | solution.py:152
  535.3 122.2 %copy-start.8 = (f32[128,4]{0,1:T(4,128)S(1)}, f32[128,4]{0,1:T(4,128)}, u32[]{:S(2)}) copy-start(f32[128,4]{0,1:T(4,128)} %param.21) | copy-start | bytes 6148
  535.3 202.6 %all-to-all-start.2 = ((bf16[32,20,2880]{2,1,0:T(8,128)(2,1)}), bf16[32,20,2880]{2,1,0:T(8,128)(2,1)}, u32[]{:S(2)}, u32[]{:S(2)}) async-start(bf16[32,20,2880]{2,1,0:T(8,128)(2,1)} %reshape_transpose_reshape.4), calls=%async_computation.2 | async-start | bytes 9043968 | tf_op jit(solution)/shard_map/all_to_all | solution.py:178
  753.8 76.9 %copy-start.1 = (bf16[1,180,2880]{2,1,0:T(8,128)(2,1)S(1)}, bf16[1,180,2880]{2,1,0:T(8,128)(2,1)}, u32[]{:S(2)}) copy-start(bf16[1,180,2880]{2,1,0:T(8,128)(2,1)} %param.23) | copy-start | bytes 3110404
  825.6 3.2 collective-permute-start
Sparse Core Ops, SparseCore 0:
  64.6 218.8 all-reduce.3
